TPU v7x, 512 devices: a whole 4x8x8 slice. The times are simulated.
512 devices in a mesh: tau: 8 (over x, core), blk: 64 (over z, y).
Axes of the slice: x: 4, y: 8, z: 8, core: 2. Of those that a mesh axis runs over, the one named last changes fastest.
Arguments:
- three_center: bfloat16 [64, 128, 128, 128], P('blk'), may hold values from -0.59765625 to 0.59765625
- green_blocks: bfloat16 [8, 512, 2048], P('tau', 'blk'), may hold values from -0.5 to 0.5
- block_owner: int32 [3072], P('blk'), may hold values from 0 to 63, as said below
- block_slot: int32 [3072], P('blk'), may hold values from 0 to 7
- fold_weights: float32 [8, 8], P(None, 'tau'), may hold values from -1 to 1
Outputs:
- chi_freq: float32 [8, 8192, 384], P('tau', 'blk')
Inputs may be any that keep to these rules, and one draw needn't show every extreme that they name: `block_owner`: among the 48 entries of each auxiliary block, no owner appears more than 2 times, and one owner appears exactly 2 times in the entries of every auxiliary block.
All inputs are finite; a program needn't handle non-finite values.
Results may differ from a plain program's by a relative error of at most 0.0041.
Values may be sent and summed in bfloat16 or wider, within the bound.
No kernel may reach another device: no remote copies, remote signals or barrier semaphores. Data moves between devices by JAX's collectives and lax.ppermute only.
A program may use at most 128 MiB of HBM per device.

v0:
```python
import jax
import jax.numpy as jnp
from jax import lax
from jax.sharding import PartitionSpec as P

AB = 32
NS = 4
HALF = 1


def from_behind(value, axis, by):
    size = lax.axis_size(axis)
    return lax.ppermute(value, axis, [(i, (i + by) % size) for i in range(size)])


def green_pair(blocks):
    blocks = blocks.reshape(NS, NS, 2, AB, AB)
    occupied = blocks[:, :, 0].transpose(0, 2, 1, 3).reshape(NS * AB, NS * AB)
    virtual = blocks[:, :, 1].transpose(0, 2, 1, 3).reshape(NS * AB, NS * AB)
    return (occupied, virtual)


def transform(occupied, virtual, source):
    region = source.shape[0]
    aux_width = source.shape[2]
    halfway = jnp.einsum("sn,mnb->msb", virtual, source, preferred_element_type=jnp.float32).astype(
        jnp.bfloat16
    )
    image_block = jnp.dot(
        occupied, halfway.reshape(region, region * aux_width), preferred_element_type=jnp.float32
    )
    return image_block.astype(jnp.bfloat16).reshape(region, region, aux_width)


def pair_block(partner, image_block):
    region = partner.shape[0]
    aux_width = partner.shape[2]
    flat_image = image_block.reshape(region * region, aux_width)
    flat_partner = partner.reshape(region * region, aux_width)
    product = lax.dot_general(
        flat_image, flat_partner, (((0,), (0,)), ((), ())), preferred_element_type=jnp.float32
    )
    return -2.0 * product


def local(three_center, green_blocks, block_owner, block_slot, fold_weights):
    source = three_center[0]
    local_table = green_blocks[0]
    devices = lax.axis_size("blk")
    requests = block_owner.shape[0]
    per_slot = NS * NS
    capacity = 2 * ((requests + devices - 1) // devices)
    owner_match = (block_owner[:, None] == jnp.arange(devices, dtype=jnp.int32)[None, :]).astype(
        jnp.int32
    )
    position = jnp.sum(jnp.cumsum(owner_match, axis=0) * owner_match, axis=1) - 1
    outgoing = jnp.zeros((devices, capacity), jnp.int32).at[block_owner, position].set(block_slot)
    found_blocks = jnp.take(
        local_table,
        lax.all_to_all(outgoing, "blk", split_axis=0, concat_axis=0, tiled=True),
        axis=0,
    )
    replies = lax.all_to_all(found_blocks, "blk", split_axis=0, concat_axis=0, tiled=True)
    fetched = replies[block_owner, position]
    partners_total = 2 * HALF + 1
    pieces = []
    for slot_index in range(partners_total):
        occupied, virtual = green_pair(fetched[slot_index * per_slot : (slot_index + 1) * per_slot])
        image_block = transform(occupied, virtual, source)
        if slot_index == HALF:
            partner = source
        else:
            partner = from_behind(source, "blk", HALF - slot_index)
        pieces.append(pair_block(partner, image_block))
    chi_time = jnp.concatenate(pieces, axis=1)
    column_weights = fold_weights[:, 0]
    return lax.psum_scatter(
        column_weights[:, None, None] * chi_time[None], "tau", scatter_dimension=0, tiled=True
    )


def solution(mesh):
    return jax.shard_map(
        local,
        mesh=mesh,
        in_specs=(
            P("blk", None, None, None),
            P("tau", "blk", None),
            P("blk"),
            P("blk"),
            P(None, "tau"),
        ),
        out_specs=P("tau", "blk", None),
        check_vma=False,
    )
```

profile of v0, /device:TPU:56, one launch (start us, length us, event | category | flops | bytes accessed | tf_op | source)
XLA Modules:
  0.0 262.6 jit_solution(15727461402452106913)
XLA Ops:
  6.5 0.7 fusion.6
  7.3 0.8 select_reduce_fusion
  8.2 0.7 fusion.10
  8.9 4.4 %scatter_fusion = s32[64,2]{0,1:T(2,128)S(1)} fusion(s32[64,2]{0,1:T(2,128)S(1)} %broadcast_in_dim.24, s32[48]{0:T(128)S(1)} %get-tuple-element.15, s32[48]{0:T(128)} %param.8), kind=kCustom, calls=%fused_computation.2 | custom fusion | bytes 960 | tf_op jit(solution)/shard_map/scatter | solution.py:57
  13.4 25.3 %all_to_all.20 = s32[64,1,2]{2,1,0:T(1,128)S(1)} all-to-all(s32[64,1,2]{2,1,0:T(1,128)S(1)} %copy.21), channel_id=1, replica_groups=mesh['tau'=8,'blk'=64] {'blk'}, dimensions={0} | all-to-all | bytes 1024 | tf_op jit(solution)/shard_map/all_to_all | solution.py:60
  38.9 0.1 reshape.117
  39.1 0.9 gather_fusion
  40.0 0.3 reshape.116
  40.5 1.4 broadcast_select_fusion
  41.9 6.9 %all-to-all-start.1 = ((bf16[64,2,2048]{2,1,0:T(2,128)(2,1)}), bf16[64,2,2048]{2,1,0:T(2,128)(2,1)S(1)}, u32[]{:S(2)}, u32[]{:S(2)}) async-start(bf16[64,2,2048]{2,1,0:T(2,128)(2,1)} %broadcast_select_fusion), calls=%async_computation.1 | async-start | bytes 1048576 | tf_op jit(solution)/shard_map/all_to_all | solution.py:63
  48.9 3.4 %collective-permute-start = (bf16[128,128,128]{2,1,0:T(8,128)(2,1)}, bf16[128,128,128]{2,1,0:T(8,128)(2,1)}, u32[]{:S(2)}, u32[]{:S(2)}) collective-permute-start(bf16[128,128,128]{2,1,0:T(8,128)(2,1)} %bitcast.106), channel_id=1, source_target_pairs={{0,1},{1,2},{2,3},{3,4},{4,5},{5,6},{6,7},{7,8},{8,9},{9,10},{10,1... | collective-permute-start | bytes 12582920 | tf_op jit(solution)/shard_map/ppermute | solution.py:13
  52.3 2.5 collective-permute-start.1
  54.8 96.3 %all-to-all-done.1 = bf16[64,2,2048]{2,1,0:T(2,128)(2,1)S(1)} async-done(((bf16[64,2,2048]{2,1,0:T(2,128)(2,1)}), bf16[64,2,2048]{2,1,0:T(2,128)(2,1)S(1)}, u32[]{:S(2)}, u32[]{:S(2)}) %all-to-all-start.1) | async-done | bytes 524320 | tf_op jit(solution)/shard_map/all_to_all | solution.py:63
  151.1 1.2 gather_fusion.1
  152.3 0.2 reshape.101
  152.6 0.1 copy_bitcast_fusion.4
  152.8 5.4 %convolution_convert_fusion.5 = bf16[128,128,128]{2,0,1:T(8,128)(2,1)} fusion(bf16[128,128,1]{1,0,2:T(8,128)(2,1)S(1)} %reshape.136, bf16[1,128,128,128]{3,2,1,0:T(8,128)(2,1)} %param.5), kind=kOutput, calls=%fused_computation.14 | convolution fusion | flops 538968064 | bytes 8421376 | tf_op jit(solution)/shard_map/sn,mnb->msb/dot_general | solution.py:26
  158.3 7.3 %convolution_convert_fusion.2 = bf16[128,16384]{1,0:T(8,128)(2,1)} fusion(bf16[128,128]{1,0:T(8,128)(2,1)S(1)} %reshape.102, bf16[16,8,128,128]{3,2,1,0:T(8,128)(2,1)} %bitcast.109), kind=kOutput, calls=%fused_computation.5 | convolution fusion | flops 538968064 | bytes 8421376 | tf_op jit(solution)/shard_map/dot_general | solution.py:29
  165.7 7.4 %reshape_reshape.9 = bf16[16384,128]{1,0:T(8,128)(2,1)} reshape(bf16[128,16384]{1,0:T(8,128)(2,1)} %convolution_convert_fusion.2) | data formatting | bytes 8388608 | tf_op jit(solution)/shard_map/reshape;reshape | solution.py:38
  173.1 0.2 reshape.110
  173.7 3.4 %convolution_convert_fusion.3 = bf16[128,128,128]{2,0,1:T(8,128)(2,1)S(1)} fusion(bf16[128,128,1]{1,0,2:T(8,128)(2,1)S(1)} %reshape.138, bf16[1,128,128,128]{3,2,1,0:T(8,128)(2,1)} %param.5), kind=kOutput, calls=%fused_computation.12 | convolution fusion | flops 538968064 | bytes 8421376 | tf_op jit(solution)/shard_map/sn,mnb->msb/dot_general | solution.py:26
  177.1 5.2 %convolution_convert_fusion = bf16[128,16384]{1,0:T(8,128)(2,1)} fusion(bf16[128,128]{1,0:T(8,128)(2,1)S(1)} %reshape.111, bf16[16,8,128,128]{3,2,1,0:T(8,128)(2,1)S(1)} %bitcast.110), kind=kOutput, calls=%fused_computation.3 | convolution fusion | flops 538968064 | bytes 8421376 | tf_op jit(solution)/shard_map/dot_general | solution.py:29
  182.3 7.4 %reshape_reshape.11 = bf16[16384,128]{1,0:T(8,128)(2,1)} reshape(bf16[128,16384]{1,0:T(8,128)(2,1)} %convolution_convert_fusion) | data formatting | bytes 8388608 | tf_op jit(solution)/shard_map/reshape;reshape | solution.py:38
  189.7 0.2 reshape.106
  190.3 3.4 %convolution_convert_fusion.4 = bf16[128,128,128]{2,0,1:T(8,128)(2,1)S(1)} fusion(bf16[128,128,1]{1,0,2:T(8,128)(2,1)S(1)} %reshape.137, bf16[1,128,128,128]{3,2,1,0:T(8,128)(2,1)} %param.5), kind=kOutput, calls=%fused_computation.13 | convolution fusion | flops 538968064 | bytes 8421376 | tf_op jit(solution)/shard_map/sn,mnb->msb/dot_general | solution.py:26
  193.7 5.2 %convolution_convert_fusion.1 = bf16[128,16384]{1,0:T(8,128)(2,1)} fusion(bf16[128,128]{1,0:T(8,128)(2,1)S(1)} %reshape.107, bf16[16,8,128,128]{3,2,1,0:T(8,128)(2,1)S(1)} %bitcast.111), kind=kOutput, calls=%fused_computation.4 | convolution fusion | flops 538968064 | bytes 8421376 | tf_op jit(solution)/shard_map/dot_general | solution.py:29
  198.9 7.5 %reshape_reshape.10 = bf16[16384,128]{1,0:T(8,128)(2,1)} reshape(bf16[128,16384]{1,0:T(8,128)(2,1)} %convolution_convert_fusion.1) | data formatting | bytes 8388608 | tf_op jit(solution)/shard_map/reshape;reshape | solution.py:38
  206.4 4.9 %convolution_multiply_fusion.1 = f32[128,128]{0,1:T(8,128)S(1)} fusion(bf16[16384,128]{1,0:T(8,128)(2,1)} %reshape_reshape.10, bf16[16384,128]{1,0:T(8,128)(2,1)} %bitcast.108), kind=kOutput, calls=%fused_computation.16 | convolution fusion | flops 536887296 | bytes 8454144 | tf_op jit(solution)/shard_map/dot_general | solution.py:40
  211.3 3.7 %convolution_multiply_fusion.2 = f32[128,128]{0,1:T(8,128)S(1)} fusion(bf16[16384,128]{1,0:T(8,128)(2,1)S(1)} %copy-done.1, bf16[16384,128]{1,0:T(8,128)(2,1)} %bitcast.16), kind=kOutput, calls=%fused_computation.17 | convolution fusion | flops 536887296 | bytes 8454144 | tf_op jit(solution)/shard_map/dot_general | solution.py:40
  215.0 3.5 %convolution_multiply_fusion = f32[128,128]{0,1:T(8,128)S(1)} fusion(bf16[16384,128]{1,0:T(8,128)(2,1)S(1)} %copy-done.2, bf16[16384,128]{1,0:T(8,128)(2,1)} %bitcast.28), kind=kOutput, calls=%fused_computation.15 | convolution fusion | flops 536887296 | bytes 8454144 | tf_op jit(solution)/shard_map/dot_general | solution.py:40
  218.7 1.3 broadcast_multiply_fusion
  220.1 35.6 %reduce-scatter.2.cloned.1.call-done = f32[1,128,384]{2,1,0:T(8,128)} async-done(((f32[8,128,384]{2,1,0:T(8,128)}), f32[1,128,384]{2,1,0:T(8,128)}) %reduce-scatter.2.cloned.1.call-update) | async-done | bytes 196624 | tf_op jit(solution)/shard_map/reduce_scatter | solution.py:77
  (35 shorter events, 1.8 us)
Async XLA Ops:
  6.5 32.5 %copy-start = (bf16[1,8,2048]{2,1,0:T(8,128)(2,1)S(1)}, bf16[1,8,2048]{2,1,0:T(8,128)(2,1)}, u32[]{:S(2)}) copy-start(bf16[1,8,2048]{2,1,0:T(8,128)(2,1)} %param.6) | copy-start | bytes 98308
  41.9 109.2 %all-to-all-start.1 = ((bf16[64,2,2048]{2,1,0:T(2,128)(2,1)}), bf16[64,2,2048]{2,1,0:T(2,128)(2,1)S(1)}, u32[]{:S(2)}, u32[]{:S(2)}) async-start(bf16[64,2,2048]{2,1,0:T(2,128)(2,1)} %broadcast_select_fusion), calls=%async_computation.1 | async-start | bytes 1048576 | tf_op jit(solution)/shard_map/all_to_all | solution.py:63
  48.8 206.9 %reduce-scatter.2.cloned.1.call-start = ((), (), s32[]{:S(2)}) async-start(), calls=%async_computation.3 | async-start | bytes 1769472 | tf_op jit(solution)/shard_map/reduce_scatter | solution.py:77
  48.9 162.4 %collective-permute-start = (bf16[128,128,128]{2,1,0:T(8,128)(2,1)}, bf16[128,128,128]{2,1,0:T(8,128)(2,1)}, u32[]{:S(2)}, u32[]{:S(2)}) collective-permute-start(bf16[128,128,128]{2,1,0:T(8,128)(2,1)} %bitcast.106), channel_id=1, source_target_pairs={{0,1},{1,2},{2,3},{3,4},{4,5},{5,6},{6,7},{7,8},{8,9},{9,10},{10,1... | collective-permute-start | bytes 12582920 | tf_op jit(solution)/shard_map/ppermute | solution.py:13
  52.3 162.7 %collective-permute-start.1 = (bf16[128,128,128]{2,1,0:T(8,128)(2,1)}, bf16[128,128,128]{2,1,0:T(8,128)(2,1)}, u32[]{:S(2)}, u32[]{:S(2)}) collective-permute-start(bf16[128,128,128]{2,1,0:T(8,128)(2,1)} %bitcast.107), channel_id=1, source_target_pairs={{0,63},{1,0},{2,1},{3,2},{4,3},{5,4},{6,5},{7,6},{8,7},{9,8},{10,9... | collective-permute-start | bytes 12582920 | tf_op jit(solution)/shard_map/ppermute | solution.py:13
  206.4 5.0 %copy-start.1 = (bf16[16384,128]{1,0:T(8,128)(2,1)S(1)}, bf16[16384,128]{1,0:T(8,128)(2,1)}, u32[]{:S(2)}) copy-start(bf16[16384,128]{1,0:T(8,128)(2,1)} %reshape_reshape.9) | copy-start | bytes 12582916
  211.3 3.7 %copy-start.2 = (bf16[16384,128]{1,0:T(8,128)(2,1)S(1)}, bf16[16384,128]{1,0:T(8,128)(2,1)}, u32[]{:S(2)}) copy-start(bf16[16384,128]{1,0:T(8,128)(2,1)} %reshape_reshape.11) | copy-start | bytes 12582916
  215.0 3.7 %copy-start.3 = (f32[8,1]{0,1:T(1,128)S(1)}, f32[8,1]{0,1:T(1,128)}, u32[]{:S(2)}) copy-start(f32[8,1]{0,1:T(1,128)} %param.9) | copy-start | bytes 100
Sparse Core Ops, SparseCore 0:
  220.2 35.4 reduce-scatter.1
where the time goes:
time: 264 us; the launch traced here: 263 us
  waiting for transfers between devices  132 us (50%)
  matrix products  42 us (16%)
  local copies, waits for them, and re-layouts  31.6 us (12%)
  blocking collectives  25.3 us (10%)
  between operations  13.7 us (5%)
  starting transfers between devices  12.8 us (5%)
  other arithmetic  5.07 us (2%)
    all_to_all x1, waiting for transfers between devices, local(): lax.all_to_all(found_blocks, 'blk', split_axis=0, concat_axis=0, tiled=True)  96.3 us
    reduce_scatter x1, waiting for transfers between devices, local(): lax.psum_scatter(column_weights[:, None, None] * chi_time[None], 'tau', s...  35.6 us
    all_to_all x1, blocking collectives, local(): lax.all_to_all(outgoing, 'blk', split_axis=0, concat_axis=0, tiled=True)  25.3 us
    another operation x3, local copies, waits for them, and re-layouts, pair_block(): flat_image = image_block.reshape(region * region, aux_width)  22.2 us
    dot_general x3, matrix products, transform(): jnp.dot(occupied, halfway.reshape(region, region * aux_width), preferred_...  17.6 us
    dot_general x3, matrix products, transform(): jnp.einsum('sn,mnb->msb', virtual, source, preferred_element_type=jnp.flo...  12.2 us
    dot_general x3, matrix products, pair_block(): lax.dot_general(flat_image, flat_partner, (((0,), (0,)), ((), ())), prefe...  12.1 us
    all_to_all x1, starting transfers between devices, local(): lax.all_to_all(found_blocks, 'blk', split_axis=0, concat_axis=0, tiled=True)  6.95 us
  transfers between devices with their start and end apart: 4, of which 2 were waited for; matrix products, arithmetic and copies ran while one was open for 24% of the time, Pallas kernels for 0%

commit v1 on v0

--- a/solution.py
+++ b/solution.py
@@ -74,9 +74,9 @@
         pieces.append(pair_block(partner, image_block))
     chi_time = jnp.concatenate(pieces, axis=1)
     column_weights = fold_weights[:, 0]
-    return lax.psum_scatter(
-        column_weights[:, None, None] * chi_time[None], "tau", scatter_dimension=0, tiled=True
-    )
+    weighted = column_weights[:, None, None] * chi_time[None]
+    received = lax.all_to_all(weighted, "tau", split_axis=0, concat_axis=0, tiled=True)
+    return jnp.sum(received, axis=0, keepdims=True)
 
 
 def solution(mesh):

time: 264 us -> 240 us (0.909)
  waiting for transfers between devices: 132 us -> 96.4 us
  blocking collectives: 25.3 us -> 51 us
  between operations: 13.7 us -> 0.32 us
    reduce_scatter x1 -> x0, waiting for transfers between devices: 35.6 us -> none  [local(): lax.psum_scatter(column_weights[:, None, None] * chi_time[None], 'tau', s...]
    all_to_all x0 -> x1, blocking collectives: none -> 25.7 us  [local(): lax.all_to_all(weighted, 'tau', split_axis=0, concat_axis=0, tiled=True)]
  transfers between devices with their start and end apart: 4 -> 3, of which waited for: 2 -> 1; matrix products, arithmetic and copies ran while one was open for 24% -> 27% of each run, Pallas kernels for 0% -> 0%
where the time goes in v1:
time: 240 us; the launch traced here: 239 us
  waiting for transfers between devices  96.4 us (40%)
  blocking collectives  51 us (21%)
  matrix products  42 us (18%)
  local copies, waits for them, and re-layouts  31.6 us (13%)
  starting transfers between devices  12.8 us (5%)
  other arithmetic  4.68 us (2%)
    all_to_all x1, waiting for transfers between devices, local(): lax.all_to_all(found_blocks, 'blk', split_axis=0, concat_axis=0, tiled=True)  96.4 us
    all_to_all x1, blocking collectives, local(): lax.all_to_all(weighted, 'tau', split_axis=0, concat_axis=0, tiled=True)  25.7 us
    all_to_all x1, blocking collectives, local(): lax.all_to_all(outgoing, 'blk', split_axis=0, concat_axis=0, tiled=True)  25.3 us
    another operation x3, local copies, waits for them, and re-layouts, pair_block(): flat_image = image_block.reshape(region * region, aux_width)  22.2 us
    dot_general x3, matrix products, transform(): jnp.dot(occupied, halfway.reshape(region, region * aux_width), preferred_...  17.6 us
    dot_general x3, matrix products, transform(): jnp.einsum('sn,mnb->msb', virtual, source, preferred_element_type=jnp.flo...  12.2 us
    dot_general x3, matrix products, pair_block(): lax.dot_general(flat_image, flat_partner, (((0,), (0,)), ((), ())), prefe...  12.1 us
    all_to_all x1, starting transfers between devices, local(): lax.all_to_all(found_blocks, 'blk', split_axis=0, concat_axis=0, tiled=True)  6.95 us
  transfers between devices with their start and end apart: 3, of which 1 were waited for; matrix products, arithmetic and copies ran while one was open for 27% of the time, Pallas kernels for 0%

profile of v1, /device:TPU:56, one launch (start us, length us, event | category | flops | bytes accessed | tf_op | source)
XLA Modules:
  0.0 238.8 jit_solution(7750372195115575420)
XLA Ops:
  0.0 0.7 fusion.6
  0.8 0.8 select_reduce_fusion
  1.6 0.7 fusion.10
  2.3 4.4 %scatter_fusion = s32[64,2]{0,1:T(2,128)S(1)} fusion(s32[64,2]{0,1:T(2,128)S(1)} %broadcast_in_dim.27, s32[48]{0:T(128)S(1)} %get-tuple-element.15, s32[48]{0:T(128)} %param.8), kind=kCustom, calls=%fused_computation.2 | custom fusion | bytes 960 | tf_op jit(solution)/shard_map/scatter | solution.py:57
  6.9 25.3 %all_to_all.25 = s32[64,1,2]{2,1,0:T(1,128)S(1)} all-to-all(s32[64,1,2]{2,1,0:T(1,128)S(1)} %copy.33), channel_id=1, replica_groups=mesh['tau'=8,'blk'=64] {'blk'}, dimensions={0} | all-to-all | bytes 1024 | tf_op jit(solution)/shard_map/all_to_all | solution.py:60
  32.4 0.1 reshape.117
  32.6 0.9 gather_fusion
  33.5 0.3 reshape.116
  34.0 1.4 broadcast_select_fusion
  35.4 6.9 %all-to-all-start.1 = ((bf16[64,2,2048]{2,1,0:T(2,128)(2,1)}), bf16[64,2,2048]{2,1,0:T(2,128)(2,1)S(1)}, u32[]{:S(2)}, u32[]{:S(2)}) async-start(bf16[64,2,2048]{2,1,0:T(2,128)(2,1)} %broadcast_select_fusion), calls=%async_computation.1 | async-start | bytes 1048576 | tf_op jit(solution)/shard_map/all_to_all | solution.py:63
  42.3 3.4 %collective-permute-start = (bf16[128,128,128]{2,1,0:T(8,128)(2,1)}, bf16[128,128,128]{2,1,0:T(8,128)(2,1)}, u32[]{:S(2)}, u32[]{:S(2)}) collective-permute-start(bf16[128,128,128]{2,1,0:T(8,128)(2,1)} %bitcast.107), channel_id=1, source_target_pairs={{0,1},{1,2},{2,3},{3,4},{4,5},{5,6},{6,7},{7,8},{8,9},{9,10},{10,1... | collective-permute-start | bytes 12582920 | tf_op jit(solution)/shard_map/ppermute | solution.py:13
  45.7 2.5 %collective-permute-start.1 = (bf16[128,128,128]{2,1,0:T(8,128)(2,1)}, bf16[128,128,128]{2,1,0:T(8,128)(2,1)}, u32[]{:S(2)}, u32[]{:S(2)}) collective-permute-start(bf16[128,128,128]{2,1,0:T(8,128)(2,1)} %bitcast.108), channel_id=1, source_target_pairs={{0,63},{1,0},{2,1},{3,2},{4,3},{5,4},{6,5},{7,6},{8,7},{9,8},{10,9... | collective-permute-start | bytes 12582920 | tf_op jit(solution)/shard_map/ppermute | solution.py:13
  48.2 96.4 %all-to-all-done.1 = bf16[64,2,2048]{2,1,0:T(2,128)(2,1)S(1)} async-done(((bf16[64,2,2048]{2,1,0:T(2,128)(2,1)}), bf16[64,2,2048]{2,1,0:T(2,128)(2,1)S(1)}, u32[]{:S(2)}, u32[]{:S(2)}) %all-to-all-start.1) | async-done | bytes 524320 | tf_op jit(solution)/shard_map/all_to_all | solution.py:63
  144.6 1.2 gather_fusion.1
  145.8 0.2 reshape.101
  146.3 5.4 %convolution_convert_fusion.5 = bf16[128,128,128]{2,0,1:T(8,128)(2,1)} fusion(bf16[128,128,1]{1,0,2:T(8,128)(2,1)S(1)} %reshape.136, bf16[1,128,128,128]{3,2,1,0:T(8,128)(2,1)} %param.5), kind=kOutput, calls=%fused_computation.14 | convolution fusion | flops 538968064 | bytes 8421376 | tf_op jit(solution)/shard_map/sn,mnb->msb/dot_general | solution.py:26
  151.8 7.3 %convolution_convert_fusion.2 = bf16[128,16384]{1,0:T(8,128)(2,1)} fusion(bf16[128,128]{1,0:T(8,128)(2,1)S(1)} %reshape.102, bf16[16,8,128,128]{3,2,1,0:T(8,128)(2,1)} %bitcast.110), kind=kOutput, calls=%fused_computation.5 | convolution fusion | flops 538968064 | bytes 8421376 | tf_op jit(solution)/shard_map/dot_general | solution.py:29
  159.2 7.4 %reshape_reshape.9 = bf16[16384,128]{1,0:T(8,128)(2,1)} reshape(bf16[128,16384]{1,0:T(8,128)(2,1)} %convolution_convert_fusion.2) | data formatting | bytes 8388608 | tf_op jit(solution)/shard_map/reshape;reshape | solution.py:38
  166.5 0.2 reshape.110
  167.2 3.4 %convolution_convert_fusion.3 = bf16[128,128,128]{2,0,1:T(8,128)(2,1)S(1)} fusion(bf16[128,128,1]{1,0,2:T(8,128)(2,1)S(1)} %reshape.138, bf16[1,128,128,128]{3,2,1,0:T(8,128)(2,1)} %param.5), kind=kOutput, calls=%fused_computation.12 | convolution fusion | flops 538968064 | bytes 8421376 | tf_op jit(solution)/shard_map/sn,mnb->msb/dot_general | solution.py:26
  170.6 5.2 %convolution_convert_fusion = bf16[128,16384]{1,0:T(8,128)(2,1)} fusion(bf16[128,128]{1,0:T(8,128)(2,1)S(1)} %reshape.111, bf16[16,8,128,128]{3,2,1,0:T(8,128)(2,1)S(1)} %bitcast.111), kind=kOutput, calls=%fused_computation.3 | convolution fusion | flops 538968064 | bytes 8421376 | tf_op jit(solution)/shard_map/dot_general | solution.py:29
  175.8 7.4 %reshape_reshape.11 = bf16[16384,128]{1,0:T(8,128)(2,1)} reshape(bf16[128,16384]{1,0:T(8,128)(2,1)} %convolution_convert_fusion) | data formatting | bytes 8388608 | tf_op jit(solution)/shard_map/reshape;reshape | solution.py:38
  183.2 0.2 reshape.106
  183.8 3.4 %convolution_convert_fusion.4 = bf16[128,128,128]{2,0,1:T(8,128)(2,1)S(1)} fusion(bf16[128,128,1]{1,0,2:T(8,128)(2,1)S(1)} %reshape.137, bf16[1,128,128,128]{3,2,1,0:T(8,128)(2,1)} %param.5), kind=kOutput, calls=%fused_computation.13 | convolution fusion | flops 538968064 | bytes 8421376 | tf_op jit(solution)/shard_map/sn,mnb->msb/dot_general | solution.py:26
  187.2 5.2 %convolution_convert_fusion.1 = bf16[128,16384]{1,0:T(8,128)(2,1)} fusion(bf16[128,128]{1,0:T(8,128)(2,1)S(1)} %reshape.107, bf16[16,8,128,128]{3,2,1,0:T(8,128)(2,1)S(1)} %bitcast.112), kind=kOutput, calls=%fused_computation.4 | convolution fusion | flops 538968064 | bytes 8421376 | tf_op jit(solution)/shard_map/dot_general | solution.py:29
  192.4 7.4 %reshape_reshape.10 = bf16[16384,128]{1,0:T(8,128)(2,1)} reshape(bf16[128,16384]{1,0:T(8,128)(2,1)} %convolution_convert_fusion.1) | data formatting | bytes 8388608 | tf_op jit(solution)/shard_map/reshape;reshape | solution.py:38
  199.8 4.9 %convolution_multiply_fusion.1 = f32[128,128]{0,1:T(8,128)S(1)} fusion(bf16[16384,128]{1,0:T(8,128)(2,1)} %reshape_reshape.10, bf16[16384,128]{1,0:T(8,128)(2,1)} %bitcast.109), kind=kOutput, calls=%fused_computation.16 | convolution fusion | flops 536887296 | bytes 8454144 | tf_op jit(solution)/shard_map/dot_general | solution.py:40
  204.8 3.7 %convolution_multiply_fusion.2 = f32[128,128]{0,1:T(8,128)S(1)} fusion(bf16[16384,128]{1,0:T(8,128)(2,1)S(1)} %copy-done.1, bf16[16384,128]{1,0:T(8,128)(2,1)} %bitcast.16), kind=kOutput, calls=%fused_computation.17 | convolution fusion | flops 536887296 | bytes 8454144 | tf_op jit(solution)/shard_map/dot_general | solution.py:40
  208.5 3.5 %convolution_multiply_fusion = f32[128,128]{0,1:T(8,128)S(1)} fusion(bf16[16384,128]{1,0:T(8,128)(2,1)S(1)} %copy-done.2, bf16[16384,128]{1,0:T(8,128)(2,1)} %bitcast.28), kind=kOutput, calls=%fused_computation.15 | convolution fusion | flops 536887296 | bytes 8454144 | tf_op jit(solution)/shard_map/dot_general | solution.py:40
  212.2 0.2 broadcast_multiply_fusion
  212.4 25.7 %all_to_all.26 = f32[8,128,384]{2,1,0:T(8,128)S(1)} all-to-all(f32[8,128,384]{2,1,0:T(8,128)S(1)} %broadcast_multiply_fusion), channel_id=1, replica_groups=mesh['tau'=8,'blk'=64] {'tau'}, dimensions={0} | all-to-all | bytes 3145728 | tf_op jit(solution)/shard_map/all_to_all | solution.py:78
  238.1 0.8 reduce_sum.19
  (34 shorter events, 1.9 us)
Async XLA Ops:
  0.0 32.5 %copy-start = (bf16[1,8,2048]{2,1,0:T(8,128)(2,1)S(1)}, bf16[1,8,2048]{2,1,0:T(8,128)(2,1)}, u32[]{:S(2)}) copy-start(bf16[1,8,2048]{2,1,0:T(8,128)(2,1)} %param.6) | copy-start | bytes 98308
  35.4 109.2 %all-to-all-start.1 = ((bf16[64,2,2048]{2,1,0:T(2,128)(2,1)}), bf16[64,2,2048]{2,1,0:T(2,128)(2,1)S(1)}, u32[]{:S(2)}, u32[]{:S(2)}) async-start(bf16[64,2,2048]{2,1,0:T(2,128)(2,1)} %broadcast_select_fusion), calls=%async_computation.1 | async-start | bytes 1048576 | tf_op jit(solution)/shard_map/all_to_all | solution.py:63
  42.3 162.5 %collective-permute-start = (bf16[128,128,128]{2,1,0:T(8,128)(2,1)}, bf16[128,128,128]{2,1,0:T(8,128)(2,1)}, u32[]{:S(2)}, u32[]{:S(2)}) collective-permute-start(bf16[128,128,128]{2,1,0:T(8,128)(2,1)} %bitcast.107), channel_id=1, source_target_pairs={{0,1},{1,2},{2,3},{3,4},{4,5},{5,6},{6,7},{7,8},{8,9},{9,10},{10,1... | collective-permute-start | bytes 12582920 | tf_op jit(solution)/shard_map/ppermute | solution.py:13
  45.7 162.8 %collective-permute-start.1 = (bf16[128,128,128]{2,1,0:T(8,128)(2,1)}, bf16[128,128,128]{2,1,0:T(8,128)(2,1)}, u32[]{:S(2)}, u32[]{:S(2)}) collective-permute-start(bf16[128,128,128]{2,1,0:T(8,128)(2,1)} %bitcast.108), channel_id=1, source_target_pairs={{0,63},{1,0},{2,1},{3,2},{4,3},{5,4},{6,5},{7,6},{8,7},{9,8},{10,9... | collective-permute-start | bytes 12582920 | tf_op jit(solution)/shard_map/ppermute | solution.py:13
  199.8 5.0 %copy-start.1 = (bf16[16384,128]{1,0:T(8,128)(2,1)S(1)}, bf16[16384,128]{1,0:T(8,128)(2,1)}, u32[]{:S(2)}) copy-start(bf16[16384,128]{1,0:T(8,128)(2,1)} %reshape_reshape.9) | copy-start | bytes 12582916
  204.8 3.7 %copy-start.2 = (bf16[16384,128]{1,0:T(8,128)(2,1)S(1)}, bf16[16384,128]{1,0:T(8,128)(2,1)}, u32[]{:S(2)}) copy-start(bf16[16384,128]{1,0:T(8,128)(2,1)} %reshape_reshape.11) | copy-start | bytes 12582916
  208.5 3.7 %copy-start.3 = (f32[8,1]{0,1:T(1,128)S(1)}, f32[8,1]{0,1:T(1,128)}, u32[]{:S(2)}) copy-start(f32[8,1]{0,1:T(1,128)} %param.9) | copy-start | bytes 100

commit v2 on v1

--- a/solution.py
+++ b/solution.py
@@ -20,31 +20,41 @@
     return (occupied, virtual)
 
 
-def transform(occupied, virtual, source):
-    region = source.shape[0]
-    aux_width = source.shape[2]
-    halfway = jnp.einsum("sn,mnb->msb", virtual, source, preferred_element_type=jnp.float32).astype(
-        jnp.bfloat16
-    )
-    image_block = jnp.dot(
-        occupied, halfway.reshape(region, region * aux_width), preferred_element_type=jnp.float32
-    )
-    return image_block.astype(jnp.bfloat16).reshape(region, region, aux_width)
+def image_of(occupied, virtual, source_t):
+    halfway = lax.dot_general(
+        source_t, virtual, (((2,), (1,)), ((), ())), preferred_element_type=jnp.float32
+    ).astype(jnp.bfloat16)
+    image = lax.dot_general(
+        halfway, occupied, (((1,), (1,)), ((), ())), preferred_element_type=jnp.float32
+    ).astype(jnp.bfloat16)
+    return image
 
 
-def pair_block(partner, image_block):
-    region = partner.shape[0]
-    aux_width = partner.shape[2]
-    flat_image = image_block.reshape(region * region, aux_width)
-    flat_partner = partner.reshape(region * region, aux_width)
-    product = lax.dot_general(
-        flat_image, flat_partner, (((0,), (0,)), ((), ())), preferred_element_type=jnp.float32
-    )
+def pair_block(partner_t, image):
+    aux_width = image.shape[0]
+    flat_image = image.reshape(aux_width, -1)
+    flat_partner = partner_t.reshape(flat_image.shape[1], -1)
+    product = jnp.dot(flat_image, flat_partner, preferred_element_type=jnp.float32)
     return -2.0 * product
+
+
+def partner_from(own_t, by):
+    core = lax.axis_index("tau") % 2
+    half = own_t.shape[0] // 2
+    mine = lax.dynamic_slice_in_dim(own_t, core * half, half, 0)
+    fetched = from_behind(mine, "blk", by)
+    size = lax.axis_size("tau")
+    other = lax.ppermute(fetched, "tau", [(i, i ^ 1) for i in range(size)])
+    low = jnp.where(core == 0, fetched, other)
+    high = jnp.where(core == 0, other, fetched)
+    return jnp.concatenate([low, high], axis=0)
 
 
 def local(three_center, green_blocks, block_owner, block_slot, fold_weights):
     source = three_center[0]
+    source_t = jnp.transpose(source, (2, 0, 1))
+    own_t = jnp.transpose(source, (1, 0, 2))
+    partners = [partner_from(own_t, HALF - j) if j != HALF else own_t for j in range(2 * HALF + 1)]
     local_table = green_blocks[0]
     devices = lax.axis_size("blk")
     requests = block_owner.shape[0]
@@ -62,16 +72,11 @@
     )
     replies = lax.all_to_all(found_blocks, "blk", split_axis=0, concat_axis=0, tiled=True)
     fetched = replies[block_owner, position]
-    partners_total = 2 * HALF + 1
     pieces = []
-    for slot_index in range(partners_total):
+    for slot_index in range(2 * HALF + 1):
         occupied, virtual = green_pair(fetched[slot_index * per_slot : (slot_index + 1) * per_slot])
-        image_block = transform(occupied, virtual, source)
-        if slot_index == HALF:
-            partner = source
-        else:
-            partner = from_behind(source, "blk", HALF - slot_index)
-        pieces.append(pair_block(partner, image_block))
+        image = image_of(occupied, virtual, source_t)
+        pieces.append(pair_block(partners[slot_index], image))
     chi_time = jnp.concatenate(pieces, axis=1)
     column_weights = fold_weights[:, 0]
     weighted = column_weights[:, None, None] * chi_time[None]

time: 240 us -> 187 us (0.78)
  waiting for transfers between devices: 96.4 us -> 47.6 us
  blocking collectives: 51 us -> 25.7 us
  starting transfers between devices: 12.8 us -> 35.6 us
  local copies, waits for them, and re-layouts: 31.6 us -> 21.3 us
  other arithmetic: 4.68 us -> 13 us
    all_to_all x1, waiting for transfers between devices: 96.4 us -> 38 us  [local(): lax.all_to_all(found_blocks, 'blk', split_axis=0, concat_axis=0, tiled=True)]
    all_to_all x1 -> x0, blocking collectives: 25.3 us -> none  [local(): lax.all_to_all(outgoing, 'blk', split_axis=0, concat_axis=0, tiled=True)]
    another operation x3 -> x2, local copies, waits for them, and re-layouts: 22.2 us -> 4.7 us  [pair_block(): flat_image = image_block.reshape(region * region, aux_width)]
    all_to_all x0 -> x1, starting transfers between devices: none -> 15.9 us  [local(): lax.all_to_all(outgoing, 'blk', split_axis=0, concat_axis=0, tiled=True)]
    all_to_all x0 -> x1, waiting for transfers between devices: none -> 9.54 us  [local(): lax.all_to_all(outgoing, 'blk', split_axis=0, concat_axis=0, tiled=True)]
    select_n x0 -> x2, other arithmetic: none -> 8.31 us  [partner_from(): low = jnp.where(core == 0, fetched, other)]
    transpose x3 -> x2, local copies, waits for them, and re-layouts: 0.41 us -> 6.75 us  [the longest x1 6.61 us: local(): source_t = jnp.transpose(source, (2, 0, 1))]
    ppermute x0 -> x2, starting transfers between devices: none -> 4.76 us  [partner_from(): other = lax.ppermute(fetched, 'tau', [(i, i ^ 1) for i in range(size)])]
  transfers between devices with their start and end apart: 3 -> 6, of which waited for: 1 -> 2; matrix products, arithmetic and copies ran while one was open for 27% -> 29% of each run, Pallas kernels for 0% -> 0%
where the time goes in v2:
time: 187 us; the launch traced here: 186 us
  waiting for transfers between devices  47.6 us (25%)
  matrix products  42.9 us (23%)
  starting transfers between devices  35.6 us (19%)
  blocking collectives  25.7 us (14%)
  local copies, waits for them, and re-layouts  21.3 us (11%)
  other arithmetic  13 us (7%)
    all_to_all x1, waiting for transfers between devices, local(): lax.all_to_all(found_blocks, 'blk', split_axis=0, concat_axis=0, tiled=True)  38 us
    dot_general x3, matrix products, pair_block(): jnp.dot(flat_image, flat_partner, preferred_element_type=jnp.float32)  28.9 us
    all_to_all x1, blocking collectives, local(): lax.all_to_all(weighted, 'tau', split_axis=0, concat_axis=0, tiled=True)  25.7 us
    all_to_all x1, starting transfers between devices, local(): lax.all_to_all(outgoing, 'blk', split_axis=0, concat_axis=0, tiled=True)  15.9 us
    dot_general x3, matrix products, image_of(): lax.dot_general(source_t, virtual, (((2,), (1,)), ((), ())), preferred_el...  14 us
    all_to_all x1, waiting for transfers between devices, local(): lax.all_to_all(outgoing, 'blk', split_axis=0, concat_axis=0, tiled=True)  9.54 us
    select_n x2, other arithmetic, partner_from(): low = jnp.where(core == 0, fetched, other)  8.31 us
    ppermute x2, starting transfers between devices, from_behind(): lax.ppermute(value, axis, [(i, (i + by) % size) for i in range(size)])  7.94 us
  transfers between devices with their start and end apart: 6, of which 2 were waited for; matrix products, arithmetic and copies ran while one was open for 29% of the time, Pallas kernels for 0%

profile of v2, /device:TPU:56, one launch (start us, length us, event | category | flops | bytes accessed | tf_op | source)
XLA Modules:
  0.0 186.3 jit_solution(11543096478171635188)
XLA Ops:
  0.0 0.7 fusion.73
  0.8 0.8 select_reduce_fusion
  1.6 0.7 fusion.77
  2.3 4.4 %scatter_fusion = s32[64,2]{0,1:T(2,128)S(1)} fusion(s32[64,2]{0,1:T(2,128)S(1)} %broadcast_in_dim.27, s32[48]{0:T(128)S(1)} %get-tuple-element.19, s32[48]{0:T(128)} %param.8), kind=kCustom, calls=%fused_computation.2 | custom fusion | bytes 960 | tf_op jit(solution)/shard_map/scatter | solution.py:67
  6.8 0.7 copy.42
  7.5 15.9 %all-to-all-start = ((s32[64,1,2]{2,1,0:T(1,128)}), s32[64,1,2]{2,1,0:T(1,128)S(1)}, u32[]{:S(2)}, u32[]{:S(2)}) async-start(s32[64,1,2]{2,1,0:T(1,128)} %copy.42), calls=%async_computation | async-start | bytes 65536 | tf_op jit(solution)/shard_map/all_to_all | solution.py:70
  23.4 9.5 %all-to-all-done = s32[64,1,2]{2,1,0:T(1,128)S(1)} async-done(((s32[64,1,2]{2,1,0:T(1,128)}), s32[64,1,2]{2,1,0:T(1,128)S(1)}, u32[]{:S(2)}, u32[]{:S(2)}) %all-to-all-start) | async-done | bytes 544 | tf_op jit(solution)/shard_map/all_to_all | solution.py:70
  33.3 0.9 gather_fusion
  34.3 0.3 reshape.106
  34.7 1.4 broadcast_select_fusion.4
  36.1 6.9 %all-to-all-start.1 = ((bf16[64,2,2048]{2,1,0:T(2,128)(2,1)}), bf16[64,2,2048]{2,1,0:T(2,128)(2,1)S(1)}, u32[]{:S(2)}, u32[]{:S(2)}) async-start(bf16[64,2,2048]{2,1,0:T(2,128)(2,1)} %broadcast_select_fusion.4), calls=%async_computation.1 | async-start | bytes 1048576 | tf_op jit(solution)/shard_map/all_to_all | solution.py:73
  43.1 1.8 constant_dynamic-slice_fusion
  44.8 2.9 %copy.51 = bf16[1,128,64,128]{1,3,2,0:T(8,128)(2,1)} copy(bf16[1,128,64,128]{3,2,1,0:T(8,128)(2,1)S(1)} %constant_dynamic-slice_fusion) | data formatting | bytes 4194304 | tf_op jit(solution)/shard_map/dynamic-slice.1
  47.8 3.4 %collective-permute-start.2 = (bf16[64,128,128]{1,2,0:T(8,128)(2,1)}, bf16[64,128,128]{1,2,0:T(8,128)(2,1)}, u32[]{:S(2)}, u32[]{:S(2)}) collective-permute-start(bf16[64,128,128]{1,2,0:T(8,128)(2,1)} %bitcast.111), channel_id=1, source_target_pairs={{0,63},{1,0},{2,1},{3,2},{4,3},{5,4},{6,5},{7,6},{8,7},{9,8},{10,9... | collective-permute-start | bytes 6291464 | tf_op jit(solution)/shard_map/ppermute | solution.py:13
  51.1 4.6 %collective-permute-start = (bf16[64,128,128]{1,2,0:T(8,128)(2,1)}, bf16[64,128,128]{1,2,0:T(8,128)(2,1)S(1)}, u32[]{:S(2)}, u32[]{:S(2)}) collective-permute-start(bf16[64,128,128]{1,2,0:T(8,128)(2,1)} %bitcast.112), channel_id=1, source_target_pairs={{0,1},{1,2},{2,3},{3,4},{4,5},{5,6},{6,7},{7,8},{8,9},{9,10},{10,1... | collective-permute-start | bytes 6291464 | tf_op jit(solution)/shard_map/ppermute | solution.py:13
  55.7 6.6 %copy.48 = bf16[128,128,128]{2,1,0:T(8,128)(2,1)} copy(bf16[128,128,128]{0,2,1:T(8,128)(2,1)} %bitcast.109) | data formatting | bytes 8388608 | tf_op jit(solution)/shard_map/transpose | solution.py:55
  62.3 38.0 %all-to-all-done.1 = bf16[64,2,2048]{2,1,0:T(2,128)(2,1)S(1)} async-done(((bf16[64,2,2048]{2,1,0:T(2,128)(2,1)}), bf16[64,2,2048]{2,1,0:T(2,128)(2,1)S(1)}, u32[]{:S(2)}, u32[]{:S(2)}) %all-to-all-start.1) | async-done | bytes 524320 | tf_op jit(solution)/shard_map/all_to_all | solution.py:73
  100.4 1.2 gather_fusion.1
  101.6 0.2 reshape.102
  102.0 0.2 reshape.99
  102.7 2.2 %collective-permute-start.3 = (bf16[64,128,128]{1,2,0:T(8,128)(2,1)}, bf16[64,128,128]{1,2,0:T(8,128)(2,1)}, u32[]{:S(2)}, u32[]{:S(2)}) collective-permute-start(bf16[64,128,128]{1,2,0:T(8,128)(2,1)} %collective-permute-done.2), channel_id=1, source_target_pairs={{0,64},{64,0},{128,192},{192,128},{256,320},{320,256},{384,448},{4... | collective-permute-start | bytes 6291464 | tf_op jit(solution)/shard_map/ppermute | solution.py:47
  104.9 5.4 %convert_bitcast_fusion = bf16[128,128,128]{1,2,0:T(8,128)(2,1)} fusion(bf16[128,128,1]{1,0,2:T(8,128)(2,1)S(1)} %reshape.132, bf16[128,128,128]{2,1,0:T(8,128)(2,1)} %copy.48), kind=kOutput, calls=%fused_computation.20 | convolution fusion | flops 538968064 | bytes 8421376 | tf_op jit(solution)/shard_map/dot_general | solution.py:24
  110.4 3.2 %convert_bitcast_fusion.1 = bf16[128,128,128]{1,2,0:T(8,128)(2,1)} fusion(bf16[128,128,1]{1,0,2:T(8,128)(2,1)S(1)} %reshape.129, bf16[128,128,128]{2,1,0:T(8,128)(2,1)S(1)} %copy-done.1), kind=kOutput, calls=%fused_computation.22 | convolution fusion | flops 538968064 | bytes 8421376 | tf_op jit(solution)/shard_map/dot_general | solution.py:24
  113.6 2.6 %collective-permute-start.1 = (bf16[64,128,128]{1,2,0:T(8,128)(2,1)S(1)}, bf16[64,128,128]{1,2,0:T(8,128)(2,1)}, u32[]{:S(2)}, u32[]{:S(2)}) collective-permute-start(bf16[64,128,128]{1,2,0:T(8,128)(2,1)S(1)} %collective-permute-done), channel_id=1, source_target_pairs={{0,64},{64,0},{128,192},{192,128},{256,320},{320,256},{384,448},{4... | collective-permute-start | bytes 6291464 | tf_op jit(solution)/shard_map/ppermute | solution.py:47
  116.9 5.4 %convert_bitcast_fusion.2 = bf16[128,128,128]{1,2,0:T(8,128)(2,1)} fusion(bf16[128,128,1]{1,0,2:T(8,128)(2,1)S(1)} %reshape.126, bf16[128,128,128]{2,1,0:T(8,128)(2,1)} %copy.48), kind=kOutput, calls=%fused_computation.24 | convolution fusion | flops 538968064 | bytes 8421376 | tf_op jit(solution)/shard_map/dot_general | solution.py:24
  122.3 12.0 %fusion.66 = f32[128,128]{0,1:T(8,128)S(1)} fusion(bf16[128,128,128]{2,0,1:T(8,128)(2,1)} %bitcast.110, bf16[128,128,1]{1,0,2:T(8,128)(2,1)S(1)} %reshape.130, bf16[128,128,128]{1,2,0:T(8,128)(2,1)} %convert_bitcast_fusion.1), kind=kOutput, calls=%fused_computation.34 | convolution fusion | flops 1075855360 | bytes 8486912 | tf_op jit(solution)/shard_map/dot_general | solution.py:37
  134.3 4.5 %broadcast_select_fusion.1 = (bf16[64,128,128]{1,2,0:T(8,128)(2,1)}, bf16[64,128,128]{1,2,0:T(8,128)(2,1)}) fusion(bf16[64,128,128]{1,2,0:T(8,128)(2,1)} %collective-permute-done.2, bf16[64,128,128]{1,2,0:T(8,128)(2,1)} %collective-permute-done.3, pred[]{:T(512)S(6)} %eq.25), kind=kLoop, calls=%fused_computation.26 | loop fusion | flops 2097152 | bytes 8388609 | tf_op jit(solution)/shard_map/jit(_where)/select_n | solution.py:48
  138.7 8.6 %fusion.59 = f32[128,128]{0,1:T(8,128)S(1)} fusion(bf16[64,128,128]{1,2,0:T(8,128)(2,1)} %get-tuple-element.8, bf16[64,128,128]{1,2,0:T(8,128)(2,1)} %get-tuple-element.7, bf16[128,128,1]{1,0,2:T(8,128)(2,1)S(1)} %reshape.133, bf16[128,128,128]{1,2,0:T(8,128)(2,1)} %convert_bitcast_fusion), kind=kOutput, calls=%fused_computation.33 | convolution fusion | flops 1077952512 | bytes 8486912 | tf_op jit(solution)/shard_map/dot_general | solution.py:37
  147.3 3.8 %broadcast_select_fusion.3 = (bf16[64,128,128]{1,2,0:T(8,128)(2,1)}, bf16[64,128,128]{1,2,0:T(8,128)(2,1)}) fusion(bf16[64,128,128]{1,2,0:T(8,128)(2,1)S(1)} %collective-permute-done, bf16[64,128,128]{1,2,0:T(8,128)(2,1)} %collective-permute-done.1, pred[]{:T(512)S(6)} %eq.25), kind=kLoop, calls=%fused_computation.28 | loop fusion | flops 2097152 | bytes 8388609 | tf_op jit(solution)/shard_map/jit(_where)/select_n | solution.py:48
  151.2 8.4 %fusion.52 = f32[128,128]{0,1:T(8,128)S(1)} fusion(bf16[64,128,128]{1,2,0:T(8,128)(2,1)} %get-tuple-element.6, bf16[64,128,128]{1,2,0:T(8,128)(2,1)} %get-tuple-element.5, bf16[128,128,1]{1,0,2:T(8,128)(2,1)S(1)} %reshape.127, bf16[128,128,128]{1,2,0:T(8,128)(2,1)} %convert_bitcast_fusion.2), kind=kOutput, calls=%fused_computation.32 | convolution fusion | flops 1077952512 | bytes 8486912 | tf_op jit(solution)/shard_map/dot_general | solution.py:37
  159.9 25.7 %all_to_all.25 = f32[8,128,384]{2,1,0:T(8,128)S(1)} all-to-all(f32[8,128,384]{2,1,0:T(8,128)S(1)} %broadcast_multiply_fusion), channel_id=1, replica_groups=mesh['tau'=8,'blk'=64] {'tau'}, dimensions={0} | all-to-all | bytes 3145728 | tf_op jit(solution)/shard_map/all_to_all | solution.py:83
  185.6 0.8 reduce_sum.19
  (38 shorter events, 2.3 us)
Async XLA Ops:
  0.0 33.3 %copy-start = (bf16[1,8,2048]{2,1,0:T(8,128)(2,1)S(1)}, bf16[1,8,2048]{2,1,0:T(8,128)(2,1)}, u32[]{:S(2)}) copy-start(bf16[1,8,2048]{2,1,0:T(8,128)(2,1)} %param.6) | copy-start | bytes 98308
  7.5 25.5 %all-to-all-start = ((s32[64,1,2]{2,1,0:T(1,128)}), s32[64,1,2]{2,1,0:T(1,128)S(1)}, u32[]{:S(2)}, u32[]{:S(2)}) async-start(s32[64,1,2]{2,1,0:T(1,128)} %copy.42), calls=%async_computation | async-start | bytes 65536 | tf_op jit(solution)/shard_map/all_to_all | solution.py:70
  36.1 64.3 %all-to-all-start.1 = ((bf16[64,2,2048]{2,1,0:T(2,128)(2,1)}), bf16[64,2,2048]{2,1,0:T(2,128)(2,1)S(1)}, u32[]{:S(2)}, u32[]{:S(2)}) async-start(bf16[64,2,2048]{2,1,0:T(2,128)(2,1)} %broadcast_select_fusion.4), calls=%async_computation.1 | async-start | bytes 1048576 | tf_op jit(solution)/shard_map/all_to_all | solution.py:73
  47.8 55.0 %collective-permute-start.2 = (bf16[64,128,128]{1,2,0:T(8,128)(2,1)}, bf16[64,128,128]{1,2,0:T(8,128)(2,1)}, u32[]{:S(2)}, u32[]{:S(2)}) collective-permute-start(bf16[64,128,128]{1,2,0:T(8,128)(2,1)} %bitcast.111), channel_id=1, source_target_pairs={{0,63},{1,0},{2,1},{3,2},{4,3},{5,4},{6,5},{7,6},{8,7},{9,8},{10,9... | collective-permute-start | bytes 6291464 | tf_op jit(solution)/shard_map/ppermute | solution.py:13
  51.1 62.4 %collective-permute-start = (bf16[64,128,128]{1,2,0:T(8,128)(2,1)}, bf16[64,128,128]{1,2,0:T(8,128)(2,1)S(1)}, u32[]{:S(2)}, u32[]{:S(2)}) collective-permute-start(bf16[64,128,128]{1,2,0:T(8,128)(2,1)} %bitcast.112), channel_id=1, source_target_pairs={{0,1},{1,2},{2,3},{3,4},{4,5},{5,6},{6,7},{7,8},{8,9},{9,10},{10,1... | collective-permute-start | bytes 6291464 | tf_op jit(solution)/shard_map/ppermute | solution.py:13
  102.7 7.6 %copy-start.1 = (bf16[128,128,128]{2,1,0:T(8,128)(2,1)S(1)}, bf16[128,128,128]{2,1,0:T(8,128)(2,1)}, u32[]{:S(2)}) copy-start(bf16[128,128,128]{2,1,0:T(8,128)(2,1)} %copy.48) | copy-start | bytes 12582916
  102.7 31.5 %collective-permute-start.3 = (bf16[64,128,128]{1,2,0:T(8,128)(2,1)}, bf16[64,128,128]{1,2,0:T(8,128)(2,1)}, u32[]{:S(2)}, u32[]{:S(2)}) collective-permute-start(bf16[64,128,128]{1,2,0:T(8,128)(2,1)} %collective-permute-done.2), channel_id=1, source_target_pairs={{0,64},{64,0},{128,192},{192,128},{256,320},{320,256},{384,448},{4... | collective-permute-start | bytes 6291464 | tf_op jit(solution)/shard_map/ppermute | solution.py:47
  113.6 33.8 %collective-permute-start.1 = (bf16[64,128,128]{1,2,0:T(8,128)(2,1)S(1)}, bf16[64,128,128]{1,2,0:T(8,128)(2,1)}, u32[]{:S(2)}, u32[]{:S(2)}) collective-permute-start(bf16[64,128,128]{1,2,0:T(8,128)(2,1)S(1)} %collective-permute-done), channel_id=1, source_target_pairs={{0,64},{64,0},{128,192},{192,128},{256,320},{320,256},{384,448},{4... | collective-permute-start | bytes 6291464 | tf_op jit(solution)/shard_map/ppermute | solution.py:47
  151.2 8.5 %copy-start.2 = (f32[8,1]{0,1:T(1,128)S(1)}, f32[8,1]{0,1:T(1,128)}, u32[]{:S(2)}) copy-start(f32[8,1]{0,1:T(1,128)} %param.9) | copy-start | bytes 100

commit v3 on v2

--- a/solution.py
+++ b/solution.py
@@ -2,6 +2,7 @@
 import jax.numpy as jnp
 from jax import lax
 from jax.sharding import PartitionSpec as P
+
 
 AB = 32
 NS = 4
@@ -50,7 +51,7 @@
     return jnp.concatenate([low, high], axis=0)
 
 
-def local(three_center, green_blocks, block_owner, block_slot, fold_weights):
+def local_body(three_center, green_blocks, block_owner, block_slot, fold_weights):
     source = three_center[0]
     source_t = jnp.transpose(source, (2, 0, 1))
     own_t = jnp.transpose(source, (1, 0, 2))
@@ -65,11 +66,8 @@
     )
     position = jnp.sum(jnp.cumsum(owner_match, axis=0) * owner_match, axis=1) - 1
     outgoing = jnp.zeros((devices, capacity), jnp.int32).at[block_owner, position].set(block_slot)
-    found_blocks = jnp.take(
-        local_table,
-        lax.all_to_all(outgoing, "blk", split_axis=0, concat_axis=0, tiled=True),
-        axis=0,
-    )
+    asked = lax.all_to_all(outgoing, "blk", split_axis=0, concat_axis=0, tiled=True)
+    found_blocks = jnp.take(local_table, asked, axis=0)
     replies = lax.all_to_all(found_blocks, "blk", split_axis=0, concat_axis=0, tiled=True)
     fetched = replies[block_owner, position]
     pieces = []
@@ -86,7 +84,7 @@
 
 def solution(mesh):
     return jax.shard_map(
-        local,
+        local_body,
         mesh=mesh,
         in_specs=(
             P("blk", None, None, None),

time: 187 us -> 187 us (level)
  no operation moved by 1% of the time
where the time goes in v3:
time: 187 us; the launch traced here: 186 us
  waiting for transfers between devices  47.6 us (25%)
  matrix products  42.9 us (23%)
  starting transfers between devices  35.6 us (19%)
  blocking collectives  25.7 us (14%)
  local copies, waits for them, and re-layouts  21.3 us (11%)
  other arithmetic  13 us (7%)
    all_to_all x1, waiting for transfers between devices, local_body(): lax.all_to_all(found_blocks, 'blk', split_axis=0, concat_axis=0, tiled=True)  38 us
    dot_general x3, matrix products, pair_block(): jnp.dot(flat_image, flat_partner, preferred_element_type=jnp.float32)  28.9 us
    all_to_all x1, blocking collectives, local_body(): lax.all_to_all(weighted, 'tau', split_axis=0, concat_axis=0, tiled=True)  25.7 us
    all_to_all x1, starting transfers between devices, local_body(): lax.all_to_all(outgoing, 'blk', split_axis=0, concat_axis=0, tiled=True)  15.9 us
    dot_general x3, matrix products, image_of(): lax.dot_general(source_t, virtual, (((2,), (1,)), ((), ())), preferred_el...  14 us
    all_to_all x1, waiting for transfers between devices, local_body(): lax.all_to_all(outgoing, 'blk', split_axis=0, concat_axis=0, tiled=True)  9.54 us
    select_n x2, other arithmetic, partner_from(): low = jnp.where(core == 0, fetched, other)  8.31 us
    ppermute x2, starting transfers between devices, from_behind(): lax.ppermute(value, axis, [(i, (i + by) % size) for i in range(size)])  7.94 us
  transfers between devices with their start and end apart: 6, of which 2 were waited for; matrix products, arithmetic and copies ran while one was open for 29% of the time, Pallas kernels for 0%

profile of v3, /device:TPU:56, one launch (start us, length us, event | category | flops | bytes accessed | tf_op | source)
XLA Modules:
  0.0 186.3 jit_solution(11543096478171635188)
XLA Ops:
  0.0 0.7 fusion.73
  0.8 0.8 select_reduce_fusion
  1.6 0.7 fusion.77
  2.3 4.4 %scatter_fusion = s32[64,2]{0,1:T(2,128)S(1)} fusion(s32[64,2]{0,1:T(2,128)S(1)} %broadcast_in_dim.27, s32[48]{0:T(128)S(1)} %get-tuple-element.19, s32[48]{0:T(128)} %param.8), kind=kCustom, calls=%fused_computation.2 | custom fusion | bytes 960 | tf_op jit(solution)/shard_map/scatter | solution.py:68
  6.8 0.7 copy.42
  7.5 15.9 %all-to-all-start = ((s32[64,1,2]{2,1,0:T(1,128)}), s32[64,1,2]{2,1,0:T(1,128)S(1)}, u32[]{:S(2)}, u32[]{:S(2)}) async-start(s32[64,1,2]{2,1,0:T(1,128)} %copy.42), calls=%async_computation | async-start | bytes 65536 | tf_op jit(solution)/shard_map/all_to_all | solution.py:69
  23.4 9.5 %all-to-all-done = s32[64,1,2]{2,1,0:T(1,128)S(1)} async-done(((s32[64,1,2]{2,1,0:T(1,128)}), s32[64,1,2]{2,1,0:T(1,128)S(1)}, u32[]{:S(2)}, u32[]{:S(2)}) %all-to-all-start) | async-done | bytes 544 | tf_op jit(solution)/shard_map/all_to_all | solution.py:69
  33.3 0.9 gather_fusion
  34.3 0.3 reshape.106
  34.7 1.4 broadcast_select_fusion.4
  36.1 6.9 %all-to-all-start.1 = ((bf16[64,2,2048]{2,1,0:T(2,128)(2,1)}), bf16[64,2,2048]{2,1,0:T(2,128)(2,1)S(1)}, u32[]{:S(2)}, u32[]{:S(2)}) async-start(bf16[64,2,2048]{2,1,0:T(2,128)(2,1)} %broadcast_select_fusion.4), calls=%async_computation.1 | async-start | bytes 1048576 | tf_op jit(solution)/shard_map/all_to_all | solution.py:71
  43.1 1.8 constant_dynamic-slice_fusion
  44.8 2.9 %copy.51 = bf16[1,128,64,128]{1,3,2,0:T(8,128)(2,1)} copy(bf16[1,128,64,128]{3,2,1,0:T(8,128)(2,1)S(1)} %constant_dynamic-slice_fusion) | data formatting | bytes 4194304 | tf_op jit(solution)/shard_map/dynamic-slice.1
  47.8 3.4 %collective-permute-start.2 = (bf16[64,128,128]{1,2,0:T(8,128)(2,1)}, bf16[64,128,128]{1,2,0:T(8,128)(2,1)}, u32[]{:S(2)}, u32[]{:S(2)}) collective-permute-start(bf16[64,128,128]{1,2,0:T(8,128)(2,1)} %bitcast.111), channel_id=1, source_target_pairs={{0,63},{1,0},{2,1},{3,2},{4,3},{5,4},{6,5},{7,6},{8,7},{9,8},{10,9... | collective-permute-start | bytes 6291464 | tf_op jit(solution)/shard_map/ppermute | solution.py:14
  51.1 4.6 %collective-permute-start = (bf16[64,128,128]{1,2,0:T(8,128)(2,1)}, bf16[64,128,128]{1,2,0:T(8,128)(2,1)S(1)}, u32[]{:S(2)}, u32[]{:S(2)}) collective-permute-start(bf16[64,128,128]{1,2,0:T(8,128)(2,1)} %bitcast.112), channel_id=1, source_target_pairs={{0,1},{1,2},{2,3},{3,4},{4,5},{5,6},{6,7},{7,8},{8,9},{9,10},{10,1... | collective-permute-start | bytes 6291464 | tf_op jit(solution)/shard_map/ppermute | solution.py:14
  55.7 6.6 %copy.48 = bf16[128,128,128]{2,1,0:T(8,128)(2,1)} copy(bf16[128,128,128]{0,2,1:T(8,128)(2,1)} %bitcast.109) | data formatting | bytes 8388608 | tf_op jit(solution)/shard_map/transpose | solution.py:56
  62.3 38.0 %all-to-all-done.1 = bf16[64,2,2048]{2,1,0:T(2,128)(2,1)S(1)} async-done(((bf16[64,2,2048]{2,1,0:T(2,128)(2,1)}), bf16[64,2,2048]{2,1,0:T(2,128)(2,1)S(1)}, u32[]{:S(2)}, u32[]{:S(2)}) %all-to-all-start.1) | async-done | bytes 524320 | tf_op jit(solution)/shard_map/all_to_all | solution.py:71
  100.4 1.2 gather_fusion.1
  101.6 0.2 reshape.102
  102.0 0.2 reshape.99
  102.7 2.2 %collective-permute-start.3 = (bf16[64,128,128]{1,2,0:T(8,128)(2,1)}, bf16[64,128,128]{1,2,0:T(8,128)(2,1)}, u32[]{:S(2)}, u32[]{:S(2)}) collective-permute-start(bf16[64,128,128]{1,2,0:T(8,128)(2,1)} %collective-permute-done.2), channel_id=1, source_target_pairs={{0,64},{64,0},{128,192},{192,128},{256,320},{320,256},{384,448},{4... | collective-permute-start | bytes 6291464 | tf_op jit(solution)/shard_map/ppermute | solution.py:48
  104.9 5.4 %convert_bitcast_fusion = bf16[128,128,128]{1,2,0:T(8,128)(2,1)} fusion(bf16[128,128,1]{1,0,2:T(8,128)(2,1)S(1)} %reshape.132, bf16[128,128,128]{2,1,0:T(8,128)(2,1)} %copy.48), kind=kOutput, calls=%fused_computation.20 | convolution fusion | flops 538968064 | bytes 8421376 | tf_op jit(solution)/shard_map/dot_general | solution.py:25
  110.4 3.2 %convert_bitcast_fusion.1 = bf16[128,128,128]{1,2,0:T(8,128)(2,1)} fusion(bf16[128,128,1]{1,0,2:T(8,128)(2,1)S(1)} %reshape.129, bf16[128,128,128]{2,1,0:T(8,128)(2,1)S(1)} %copy-done.1), kind=kOutput, calls=%fused_computation.22 | convolution fusion | flops 538968064 | bytes 8421376 | tf_op jit(solution)/shard_map/dot_general | solution.py:25
  113.6 2.6 %collective-permute-start.1 = (bf16[64,128,128]{1,2,0:T(8,128)(2,1)S(1)}, bf16[64,128,128]{1,2,0:T(8,128)(2,1)}, u32[]{:S(2)}, u32[]{:S(2)}) collective-permute-start(bf16[64,128,128]{1,2,0:T(8,128)(2,1)S(1)} %collective-permute-done), channel_id=1, source_target_pairs={{0,64},{64,0},{128,192},{192,128},{256,320},{320,256},{384,448},{4... | collective-permute-start | bytes 6291464 | tf_op jit(solution)/shard_map/ppermute | solution.py:48
  116.9 5.4 %convert_bitcast_fusion.2 = bf16[128,128,128]{1,2,0:T(8,128)(2,1)} fusion(bf16[128,128,1]{1,0,2:T(8,128)(2,1)S(1)} %reshape.126, bf16[128,128,128]{2,1,0:T(8,128)(2,1)} %copy.48), kind=kOutput, calls=%fused_computation.24 | convolution fusion | flops 538968064 | bytes 8421376 | tf_op jit(solution)/shard_map/dot_general | solution.py:25
  122.3 12.0 %fusion.66 = f32[128,128]{0,1:T(8,128)S(1)} fusion(bf16[128,128,128]{2,0,1:T(8,128)(2,1)} %bitcast.110, bf16[128,128,1]{1,0,2:T(8,128)(2,1)S(1)} %reshape.130, bf16[128,128,128]{1,2,0:T(8,128)(2,1)} %convert_bitcast_fusion.1), kind=kOutput, calls=%fused_computation.34 | convolution fusion | flops 1075855360 | bytes 8486912 | tf_op jit(solution)/shard_map/dot_general | solution.py:38
  134.3 4.5 %broadcast_select_fusion.1 = (bf16[64,128,128]{1,2,0:T(8,128)(2,1)}, bf16[64,128,128]{1,2,0:T(8,128)(2,1)}) fusion(bf16[64,128,128]{1,2,0:T(8,128)(2,1)} %collective-permute-done.2, bf16[64,128,128]{1,2,0:T(8,128)(2,1)} %collective-permute-done.3, pred[]{:T(512)S(6)} %eq.25), kind=kLoop, calls=%fused_computation.26 | loop fusion | flops 2097152 | bytes 8388609 | tf_op jit(solution)/shard_map/jit(_where)/select_n | solution.py:49
  138.7 8.6 %fusion.59 = f32[128,128]{0,1:T(8,128)S(1)} fusion(bf16[64,128,128]{1,2,0:T(8,128)(2,1)} %get-tuple-element.8, bf16[64,128,128]{1,2,0:T(8,128)(2,1)} %get-tuple-element.7, bf16[128,128,1]{1,0,2:T(8,128)(2,1)S(1)} %reshape.133, bf16[128,128,128]{1,2,0:T(8,128)(2,1)} %convert_bitcast_fusion), kind=kOutput, calls=%fused_computation.33 | convolution fusion | flops 1077952512 | bytes 8486912 | tf_op jit(solution)/shard_map/dot_general | solution.py:38
  147.3 3.8 %broadcast_select_fusion.3 = (bf16[64,128,128]{1,2,0:T(8,128)(2,1)}, bf16[64,128,128]{1,2,0:T(8,128)(2,1)}) fusion(bf16[64,128,128]{1,2,0:T(8,128)(2,1)S(1)} %collective-permute-done, bf16[64,128,128]{1,2,0:T(8,128)(2,1)} %collective-permute-done.1, pred[]{:T(512)S(6)} %eq.25), kind=kLoop, calls=%fused_computation.28 | loop fusion | flops 2097152 | bytes 8388609 | tf_op jit(solution)/shard_map/jit(_where)/select_n | solution.py:49
  151.2 8.4 %fusion.52 = f32[128,128]{0,1:T(8,128)S(1)} fusion(bf16[64,128,128]{1,2,0:T(8,128)(2,1)} %get-tuple-element.6, bf16[64,128,128]{1,2,0:T(8,128)(2,1)} %get-tuple-element.5, bf16[128,128,1]{1,0,2:T(8,128)(2,1)S(1)} %reshape.127, bf16[128,128,128]{1,2,0:T(8,128)(2,1)} %convert_bitcast_fusion.2), kind=kOutput, calls=%fused_computation.32 | convolution fusion | flops 1077952512 | bytes 8486912 | tf_op jit(solution)/shard_map/dot_general | solution.py:38
  159.9 25.7 %all_to_all.25 = f32[8,128,384]{2,1,0:T(8,128)S(1)} all-to-all(f32[8,128,384]{2,1,0:T(8,128)S(1)} %broadcast_multiply_fusion), channel_id=1, replica_groups=mesh['tau'=8,'blk'=64] {'tau'}, dimensions={0} | all-to-all | bytes 3145728 | tf_op jit(solution)/shard_map/all_to_all | solution.py:81
  185.6 0.8 reduce_sum.19
  (38 shorter events, 2.3 us)
Async XLA Ops:
  0.0 33.3 %copy-start = (bf16[1,8,2048]{2,1,0:T(8,128)(2,1)S(1)}, bf16[1,8,2048]{2,1,0:T(8,128)(2,1)}, u32[]{:S(2)}) copy-start(bf16[1,8,2048]{2,1,0:T(8,128)(2,1)} %param.6) | copy-start | bytes 98308
  7.5 25.5 %all-to-all-start = ((s32[64,1,2]{2,1,0:T(1,128)}), s32[64,1,2]{2,1,0:T(1,128)S(1)}, u32[]{:S(2)}, u32[]{:S(2)}) async-start(s32[64,1,2]{2,1,0:T(1,128)} %copy.42), calls=%async_computation | async-start | bytes 65536 | tf_op jit(solution)/shard_map/all_to_all | solution.py:69
  36.1 64.3 %all-to-all-start.1 = ((bf16[64,2,2048]{2,1,0:T(2,128)(2,1)}), bf16[64,2,2048]{2,1,0:T(2,128)(2,1)S(1)}, u32[]{:S(2)}, u32[]{:S(2)}) async-start(bf16[64,2,2048]{2,1,0:T(2,128)(2,1)} %broadcast_select_fusion.4), calls=%async_computation.1 | async-start | bytes 1048576 | tf_op jit(solution)/shard_map/all_to_all | solution.py:71
  47.8 55.0 %collective-permute-start.2 = (bf16[64,128,128]{1,2,0:T(8,128)(2,1)}, bf16[64,128,128]{1,2,0:T(8,128)(2,1)}, u32[]{:S(2)}, u32[]{:S(2)}) collective-permute-start(bf16[64,128,128]{1,2,0:T(8,128)(2,1)} %bitcast.111), channel_id=1, source_target_pairs={{0,63},{1,0},{2,1},{3,2},{4,3},{5,4},{6,5},{7,6},{8,7},{9,8},{10,9... | collective-permute-start | bytes 6291464 | tf_op jit(solution)/shard_map/ppermute | solution.py:14
  51.1 62.4 %collective-permute-start = (bf16[64,128,128]{1,2,0:T(8,128)(2,1)}, bf16[64,128,128]{1,2,0:T(8,128)(2,1)S(1)}, u32[]{:S(2)}, u32[]{:S(2)}) collective-permute-start(bf16[64,128,128]{1,2,0:T(8,128)(2,1)} %bitcast.112), channel_id=1, source_target_pairs={{0,1},{1,2},{2,3},{3,4},{4,5},{5,6},{6,7},{7,8},{8,9},{9,10},{10,1... | collective-permute-start | bytes 6291464 | tf_op jit(solution)/shard_map/ppermute | solution.py:14
  102.7 7.6 %copy-start.1 = (bf16[128,128,128]{2,1,0:T(8,128)(2,1)S(1)}, bf16[128,128,128]{2,1,0:T(8,128)(2,1)}, u32[]{:S(2)}) copy-start(bf16[128,128,128]{2,1,0:T(8,128)(2,1)} %copy.48) | copy-start | bytes 12582916
  102.7 31.5 %collective-permute-start.3 = (bf16[64,128,128]{1,2,0:T(8,128)(2,1)}, bf16[64,128,128]{1,2,0:T(8,128)(2,1)}, u32[]{:S(2)}, u32[]{:S(2)}) collective-permute-start(bf16[64,128,128]{1,2,0:T(8,128)(2,1)} %collective-permute-done.2), channel_id=1, source_target_pairs={{0,64},{64,0},{128,192},{192,128},{256,320},{320,256},{384,448},{4... | collective-permute-start | bytes 6291464 | tf_op jit(solution)/shard_map/ppermute | solution.py:48
  113.6 33.8 %collective-permute-start.1 = (bf16[64,128,128]{1,2,0:T(8,128)(2,1)S(1)}, bf16[64,128,128]{1,2,0:T(8,128)(2,1)}, u32[]{:S(2)}, u32[]{:S(2)}) collective-permute-start(bf16[64,128,128]{1,2,0:T(8,128)(2,1)S(1)} %collective-permute-done), channel_id=1, source_target_pairs={{0,64},{64,0},{128,192},{192,128},{256,320},{320,256},{384,448},{4... | collective-permute-start | bytes 6291464 | tf_op jit(solution)/shard_map/ppermute | solution.py:48
  151.2 8.5 %copy-start.2 = (f32[8,1]{0,1:T(1,128)S(1)}, f32[8,1]{0,1:T(1,128)}, u32[]{:S(2)}) copy-start(f32[8,1]{0,1:T(1,128)} %param.9) | copy-start | bytes 100
